TPU v7x, 128 devices: a whole 4x4x4 slice. The times are simulated.
128 devices in a mesh: node: 4 (over x), ep: 32 (over y, z, core).
Axes of the slice: x: 4, y: 4, z: 4, core: 2. Of those that a mesh axis runs over, the one named last changes fastest.
Arguments:
- images: bfloat16 [128, 257, 1280], P(('node', 'ep')), may hold values from -6 to 6
- w_query: bfloat16 [1280, 1280], P(None, 'node'), may hold values from -6 to 6
- w_key: bfloat16 [1280, 1280], P(None, 'node'), may hold values from -6 to 6
- w_value: bfloat16 [1280, 1280], P(None, 'node'), may hold values from -0.15625 to 0.15625
- w_output: bfloat16 [1280, 1280], replicated, may hold values from -0.15625 to 0.15625
- router: bfloat16 [1280, 32], replicated, may hold values from -0.15625 to 0.15625
- w_in: bfloat16 [32, 1280, 5120], P('ep', None, 'node'), may hold values from -0.15625 to 0.15625
- w_out: bfloat16 [32, 5120, 1280], P('ep', 'node'), may hold values from -0.078125 to 0.078125
- routes: int32 [128, 257, 2], P(('node', 'ep')), may hold values from 0 to 31, all different within a row; in each aligned block of 257 rows (0 to 256, 257 to 513, ..., all dimensions but the last counted through in order) at most 24 rows name the same one
Outputs:
- output: bfloat16 [128, 257, 1280], P(('node', 'ep'))
Inputs may be any that keep to these rules, and one draw needn't show every extreme that they name: `routes`: the two experts of a token differ. At most 24 tokens of one image name the same expert, and in every draw some image has an expert named by exactly 24 of its tokens.
All inputs are finite; a program needn't handle non-finite values.
Results may differ from a plain program's by a relative error of at most 0.0085.
Values may be sent and summed in bfloat16 or wider, within the bound.
No kernel may reach another device: no remote copies, remote signals or barrier semaphores. Data moves between devices by JAX's collectives and lax.ppermute only.
A program may use at most 128 MiB of HBM per device.

v0:
```python
import math
import jax
import jax.numpy as jnp
from jax import lax
from jax.sharding import PartitionSpec as P

D = 1280
HEADS = 16
CAP = 24


def layer_norm(values):
    center = values - jnp.mean(values, axis=-1, keepdims=True)
    spread = jnp.mean(center * center, axis=-1, keepdims=True)
    return center * lax.rsqrt(spread + 1e-06)


def slot_table(chosen, num_experts):
    onehot = (chosen[..., None] == jnp.arange(num_experts, dtype=jnp.int32)).astype(jnp.int32)
    before = jnp.cumsum(onehot, axis=1) - onehot
    return jnp.sum(before * onehot, axis=-1)


def shards(images, w_query, w_key, w_value, w_output, router, w_in, w_out, routes):
    local_images, tokens_dev, width = images.shape
    head_size = D // HEADS
    local_heads = w_query.shape[1] // head_size
    node_count = lax.axis_size("node")
    column_count = lax.axis_size("ep")
    num_experts = router.shape[1]
    local_experts = w_in.shape[0]
    slot_count = local_images * CAP
    inputs = images.astype(jnp.float32)
    normed = layer_norm(inputs).astype(jnp.bfloat16)
    shard_rows = lax.all_gather(normed, "node", axis=0, tiled=True)
    number = shard_rows.shape[0]
    queries = jnp.einsum(
        "ctd,de->cte", shard_rows, w_query, preferred_element_type=jnp.float32
    ).astype(jnp.bfloat16)
    projected_keys = jnp.einsum(
        "ctd,de->cte", shard_rows, w_key, preferred_element_type=jnp.float32
    ).astype(jnp.bfloat16)
    projected_values = jnp.einsum(
        "ctd,de->cte", shard_rows, w_value, preferred_element_type=jnp.float32
    ).astype(jnp.bfloat16)
    query_heads = queries.reshape(number, tokens_dev, local_heads, head_size)
    key_heads = projected_keys.reshape(number, tokens_dev, local_heads, head_size)
    value_heads = projected_values.reshape(number, tokens_dev, local_heads, head_size)
    scores = jnp.einsum(
        "cqhd,ckhd->chqk", query_heads, key_heads, preferred_element_type=jnp.float32
    ) / math.sqrt(head_size)
    weights = jax.nn.softmax(scores, axis=-1).astype(jnp.bfloat16)
    mixture = jnp.einsum(
        "chqk,ckhd->cqhd", weights, value_heads, preferred_element_type=jnp.float32
    ).astype(jnp.bfloat16)
    head_results = mixture.reshape(number, tokens_dev, local_heads * head_size)
    attention = jnp.einsum(
        "itd,de->ite",
        lax.all_to_all(head_results, "node", split_axis=0, concat_axis=2, tiled=True),
        w_output,
        preferred_element_type=jnp.float32,
    )
    middle = inputs + attention
    normed_second = layer_norm(middle).astype(jnp.bfloat16)
    logits = jnp.einsum("itd,de->ite", normed_second, router, preferred_element_type=jnp.float32)
    chosen_mask = routes[..., None] == jnp.arange(num_experts, dtype=jnp.int32)
    chosen_logit = jnp.sum(jnp.where(chosen_mask, logits[:, :, None, :], jnp.float32(0.0)), axis=-1)
    gate_values = jax.nn.sigmoid(chosen_logit)
    flat_routes = routes.reshape(local_images, 2 * tokens_dev)
    slot_index = slot_table(flat_routes, num_experts)
    image_base = jnp.arange(local_images, dtype=jnp.int32)[:, None] * CAP
    position = (flat_routes * slot_count + image_base + slot_index).reshape(-1)
    token_ids = jnp.arange(local_images * 2 * tokens_dev, dtype=jnp.int32) // 2
    source = jnp.full((num_experts * slot_count,), -1, jnp.int32).at[position].set(token_ids)
    token_rows = normed_second.reshape(local_images * tokens_dev, width)
    gathered = jnp.take(token_rows, jnp.maximum(source, 0), axis=0)
    gathered = jnp.where(source[:, None] >= 0, gathered, jnp.zeros_like(gathered))
    outgoing = gathered.reshape(column_count, local_experts, slot_count, width)
    copies = jnp.broadcast_to(outgoing[None], (node_count,) + outgoing.shape)
    copies = copies.reshape(node_count * column_count, local_experts, slot_count, width)
    arrived = lax.all_to_all(copies, ("node", "ep"), split_axis=0, concat_axis=0, tiled=True)
    pre_act = jnp.einsum("lesd,edf->lesf", arrived, w_in, preferred_element_type=jnp.float32)
    hidden = jax.nn.gelu(pre_act, approximate=True).astype(jnp.bfloat16)
    partial_sum = jnp.einsum(
        "lesf,efd->lesd", hidden, w_out, preferred_element_type=jnp.float32
    ).astype(jnp.bfloat16)
    returned = lax.all_to_all(partial_sum, ("node", "ep"), split_axis=0, concat_axis=0, tiled=True)
    returned = returned.astype(jnp.float32).reshape(
        node_count, column_count, local_experts, slot_count, width
    )
    expert_result = jnp.sum(returned, axis=0).astype(jnp.bfloat16)
    result_rows = expert_result.reshape(num_experts * slot_count, width)
    picked = jnp.take(result_rows, position, axis=0).reshape(local_images, tokens_dev, 2, width)
    expert_mix = jnp.sum(gate_values[..., None] * picked.astype(jnp.float32), axis=2)
    return (middle + expert_mix).astype(jnp.bfloat16)


def solution(mesh):
    placed = (
        P(("node", "ep"), None, None),
        P(None, "node"),
        P(None, "node"),
        P(None, "node"),
        P(),
        P(),
        P("ep", None, "node"),
        P("ep", "node", None),
        P(("node", "ep"), None, None),
    )
    return jax.shard_map(
        shards, mesh=mesh, in_specs=placed, out_specs=P(("node", "ep"), None, None), check_vma=False
    )
```

profile of v0, /device:TPU:97, one launch (start us, length us, event | category | flops | bytes accessed | tf_op | source)
XLA Modules:
  0.0 396.5 jit_solution(17544285698891339135)
XLA Ops:
  15.9 4.1 %scatter_custom_fusion = s32[768]{0:T(1024)S(1)} fusion(s32[514]{0:T(1024)S(1)} %fusion.49, s32[514]{0:T(1024)S(1)} %add_select_fusion, s32[]{:T(128)} %constant.77.clone.1), kind=kCustom, calls=%fused_computation.80 | custom fusion | bytes 3076 | tf_op jit(solution)/shard_map/scatter | solution.py:74
  20.0 28.8 %all-gather.2.cloned.1.call-done = bf16[4,257,1280]{2,1,0:T(8,128)(2,1)} async-done(((bf16[1,257,1280]{2,1,0:T(8,128)(2,1)}), bf16[4,257,1280]{2,1,0:T(8,128)(2,1)}) %all-gather.2.cloned.1.call-update) | async-done | bytes 2631696 | tf_op jit(solution)/shard_map/all_gather | solution.py:35
  48.8 4.4 %convolution_convert_fusion = bf16[4,257,320]{2,1,0:T(8,128)(2,1)} fusion(bf16[4,257,1280]{2,1,0:T(8,128)(2,1)} %all-gather.2.cloned.1.call-done, bf16[1280,320]{0,1:T(8,128)(2,1)} %param.11), kind=kOutput, calls=%fused_computation.37 | convolution fusion | flops 842466560 | bytes 4108800 | tf_op jit(solution)/shard_map/ctd,de->cte/dot_general | solution.py:40
  53.2 2.3 copy.95
  55.5 4.4 %convolution_convert_fusion.2 = bf16[4,257,320]{2,1,0:T(8,128)(2,1)} fusion(bf16[4,257,1280]{2,1,0:T(8,128)(2,1)} %all-gather.2.cloned.1.call-done, bf16[1280,320]{0,1:T(8,128)(2,1)} %param.12), kind=kOutput, calls=%fused_computation.39 | convolution fusion | flops 842466560 | bytes 4108800 | tf_op jit(solution)/shard_map/ctd,de->cte/dot_general | solution.py:43
  62.2 4.4 %convolution_convert_fusion.1 = bf16[4,257,320]{2,1,0:T(8,128)(2,1)} fusion(bf16[4,257,1280]{2,1,0:T(8,128)(2,1)} %all-gather.2.cloned.1.call-done, bf16[1280,320]{0,1:T(8,128)(2,1)} %param.10), kind=kOutput, calls=%fused_computation.38 | convolution fusion | flops 842466560 | bytes 4108800 | tf_op jit(solution)/shard_map/ctd,de->cte/dot_general | solution.py:37
  66.6 2.3 copy.94
  68.9 6.5 %fusion.57 = (f32[4,4,257]{2,1,0:T(4,128)S(1)}, f32[4,4,257,257]{2,3,1,0:T(8,128)}) fusion(bf16[4,257,4,80]{1,3,2,0:T(8,128)(2,1)} %bitcast.114, bf16[4,257,4,80]{1,3,2,0:T(8,128)(2,1)} %bitcast.113), kind=kOutput, calls=%fused_computation.92 | convolution fusion | flops 172256048 | bytes 5559424 | tf_op jit(solution)/shard_map/sub | solution.py:52
  75.4 5.1 %fusion.33 = bf16[4,4,80,257]{3,2,1,0:T(8,128)(2,1)} fusion(bf16[4,257,4,80]{1,3,2,0:T(8,128)(2,1)} %bitcast.112, f32[4,4,257,257]{2,3,1,0:T(8,128)} %get-tuple-element.8, f32[4,4,257]{2,1,0:T(4,128)S(1)} %get-tuple-element.7), kind=kOutput, calls=%fused_computation.36 | convolution fusion | flops 171527968 | bytes 5559424 | tf_op jit(solution)/shard_map/chqk,ckhd->cqhd/dot_general | solution.py:53
  82.8 4.4 %all-to-all-start = ((bf16[4,257,320]{2,1,0:T(8,128)(2,1)}), bf16[4,257,320]{2,1,0:T(8,128)(2,1)}, u32[]{:S(2)}, u32[]{:S(2)}) async-start(bf16[4,257,320]{2,1,0:T(8,128)(2,1)} %copy.97), calls=%async_computation | async-start | bytes 1622016 | tf_op jit(solution)/shard_map/all_to_all | solution.py:59
  87.4 11.5 %all-to-all-done = bf16[4,257,320]{2,1,0:T(8,128)(2,1)} async-done(((bf16[4,257,320]{2,1,0:T(8,128)(2,1)}), bf16[4,257,320]{2,1,0:T(8,128)(2,1)}, u32[]{:S(2)}, u32[]{:S(2)}) %all-to-all-start) | async-done | bytes 657952 | tf_op jit(solution)/shard_map/all_to_all | solution.py:59
  98.8 2.3 copy.98
  101.2 2.5 reshape.358
  103.7 3.4 fusion.58
  109.3 6.4 %gather_fusion = bf16[768,1280]{1,0:T(8,128)(2,1)} fusion(bf16[257,1280]{1,0:T(8,128)(2,1)} %fusion.40, s32[1024]{0:T(1024)S(1)} %pad_clamp_fusion.1), kind=kCustom, calls=%fused_computation | custom fusion | bytes 3935232 | tf_op jit(solution)/shard_map/jit(_take)/gather | solution.py:76
  118.1 99.0 %all_to_all.25 = bf16[128,1,24,1280]{3,2,1,0:T(8,128)(2,1)} all-to-all(bf16[128,1,24,1280]{3,2,1,0:T(8,128)(2,1)S(1)} %bitcast.110), channel_id=1, replica_groups=mesh['node'=4,'ep'=32] {'node','ep'}, dimensions={0} | all-to-all | bytes 15728640 | tf_op jit(solution)/shard_map/all_to_all | solution.py:81
  217.1 25.9 %convert_bitcast_fusion = bf16[128,1,24,1280]{3,0,2,1:T(8,128)(2,1)} fusion(bf16[1,1280,1280]{2,1,0:T(8,128)(2,1)S(1)} %copy-done, bf16[128,1,24,1280]{3,2,1,0:T(8,128)(2,1)} %all_to_all.25, bf16[1,1280,1280]{2,1,0:T(8,128)(2,1)} %param.15), kind=kOutput, calls=%fused_computation.18 | convolution fusion | flops 20171980800 | bytes 22282240 | tf_op jit(solution)/shard_map/lesf,efd->lesd/dot_general | solution.py:84
  243.0 10.8 %copy.108 = bf16[128,1,24,1280]{3,2,1,0:T(8,128)(2,1)} copy(bf16[128,1,24,1280]{3,0,2,1:T(8,128)(2,1)} %convert_bitcast_fusion) | data formatting | bytes 15728640 | tf_op jit(solution)/shard_map/convert_element_type | solution.py:86
  253.8 10.7 %all-to-all-start.2 = ((bf16[128,1,24,1280]{3,2,1,0:T(8,128)(2,1)}), bf16[128,1,24,1280]{3,2,1,0:T(8,128)(2,1)}, u32[]{:S(2)}, u32[]{:S(2)}) async-start(bf16[128,1,24,1280]{3,2,1,0:T(8,128)(2,1)} %copy.108), calls=%async_computation.2 | async-start | bytes 15728640 | tf_op jit(solution)/shard_map/all_to_all | solution.py:87
  265.5 97.6 %all-to-all-done.2 = bf16[128,1,24,1280]{3,2,1,0:T(8,128)(2,1)} async-done(((bf16[128,1,24,1280]{3,2,1,0:T(8,128)(2,1)}), bf16[128,1,24,1280]{3,2,1,0:T(8,128)(2,1)}, u32[]{:S(2)}, u32[]{:S(2)}) %all-to-all-start.2) | async-done | bytes 7864352 | tf_op jit(solution)/shard_map/all_to_all | solution.py:87
  363.1 4.3 %bitcast_reduce_fusion = bf16[32,24,1280]{2,1,0:T(8,128)(2,1)S(1)} fusion(bf16[4,32,24,1280]{3,2,1,0:T(8,128)(2,1)} %bitcast.107), kind=kLoop, calls=%fused_computation.13 | loop fusion | flops 2949120 | bytes 9830400 | tf_op jit(solution)/shard_map/reduce_sum | solution.py:91
  367.4 3.5 gather_fusion.1
  370.9 4.1 %gather.15 = bf16[1,257,2,1280]{3,2,1,0:T(2,128)(2,1)} reshape(bf16[514,1280]{1,0:T(8,128)(2,1)} %gather_fusion.1) | data formatting | bytes 2631680 | tf_op jit(solution)/shard_map/jit(_take)/gather | solution.py:93
  375.0 13.6 %multiply_reduce_fusion.1 = f32[257,1280]{1,0:T(8,128)S(1)} fusion(bf16[1,257,2,1280]{3,2,1,0:T(2,128)(2,1)} %gather.15, pred[257,2]{1,0:T(8,128)(4,1)S(1)} %copy.105, f32[257,2]{1,0:T(8,128)S(1)} %copy.99), kind=kLoop, calls=%fused_computation.29 | loop fusion | flops 2302720 | bytes 2634250 | tf_op jit(solution)/shard_map/reduce_sum | solution.py:94
  (63 shorter events, 20.4 us)
Async XLA Ops:
  6.5 210.6 %copy-start = (bf16[1,1280,1280]{2,1,0:T(8,128)(2,1)S(1)}, bf16[1,1280,1280]{2,1,0:T(8,128)(2,1)}, u32[]{:S(2)}) copy-start(bf16[1,1280,1280]{2,1,0:T(8,128)(2,1)} %param.16) | copy-start | bytes 9830404
  6.5 5.2 %copy-start.6 = (s32[1,257,2]{1,2,0:T(2,128)S(1)}, s32[1,257,2]{1,2,0:T(2,128)}, u32[]{:S(2)}) copy-start(s32[1,257,2]{1,2,0:T(2,128)} %param.17) | copy-start | bytes 6172
  6.5 42.2 %all-gather.2.cloned.1.call-start = ((), (), s32[]{:S(2)}) async-start(), calls=%async_computation.3 | async-start | bytes 3379200 | tf_op jit(solution)/shard_map/all_gather | solution.py:35
  82.8 16.1 %all-to-all-start = ((bf16[4,257,320]{2,1,0:T(8,128)(2,1)}), bf16[4,257,320]{2,1,0:T(8,128)(2,1)}, u32[]{:S(2)}, u32[]{:S(2)}) async-start(bf16[4,257,320]{2,1,0:T(8,128)(2,1)} %copy.97), calls=%async_computation | async-start | bytes 1622016 | tf_op jit(solution)/shard_map/all_to_all | solution.py:59
  107.2 1.1 copy-start.3
  253.8 11.2 %copy-start.2 = (bf16[257,1280]{1,0:T(8,128)(2,1)S(1)}, bf16[257,1280]{1,0:T(8,128)(2,1)}, u32[]{:S(2)}) copy-start(bf16[257,1280]{1,0:T(8,128)(2,1)} %fusion.40) | copy-start | bytes 1973764
  253.8 11.2 %copy-start.5 = (bf16[1280,32]{0,1:T(8,128)(2,1)S(1)}, bf16[1280,32]{0,1:T(8,128)(2,1)}, u32[]{:S(2)}) copy-start(bf16[1280,32]{0,1:T(8,128)(2,1)} %param.14) | copy-start | bytes 245764
  253.8 109.4 %all-to-all-start.2 = ((bf16[128,1,24,1280]{3,2,1,0:T(8,128)(2,1)}), bf16[128,1,24,1280]{3,2,1,0:T(8,128)(2,1)}, u32[]{:S(2)}, u32[]{:S(2)}) async-start(bf16[128,1,24,1280]{3,2,1,0:T(8,128)(2,1)} %copy.108), calls=%async_computation.2 | async-start | bytes 15728640 | tf_op jit(solution)/shard_map/all_to_all | solution.py:87
  370.9 18.7 %copy-start.1 = (bf16[1,1280,1280]{2,1,0:T(8,128)(2,1)S(1)}, bf16[1,1280,1280]{2,1,0:T(8,128)(2,1)}, u32[]{:S(2)}) copy-start(bf16[1,1280,1280]{2,1,0:T(8,128)(2,1)} %param.16) | copy-start | bytes 9830404
  375.0 13.6 %copy-start.4 = (f32[1,257,1280]{2,1,0:T(8,128)S(1)}, f32[1,257,1280]{2,1,0:T(8,128)}, u32[]{:S(2)}) copy-start(f32[1,257,1280]{2,1,0:T(8,128)} %copy-done.3) | copy-start | bytes 3947524
Sparse Core Ops, SparseCore 0:
  11.8 36.8 all-gather.1
where the time goes:
time: 397 us; the launch traced here: 396 us
  waiting for transfers between devices  138 us (35%)
  blocking collectives  99 us (25%)
  matrix products  54.6 us (14%)
  local copies, waits for them, and re-layouts  46.4 us (12%)
  other arithmetic  29.8 us (8%)
  starting transfers between devices  15.1 us (4%)
  between operations  13.7 us (3%)
    all_to_all x1, blocking collectives, shards(): lax.all_to_all(copies, ('node', 'ep'), split_axis=0, concat_axis=0, tiled...  99 us
    all_to_all x1, waiting for transfers between devices, shards(): lax.all_to_all(partial_sum, ('node', 'ep'), split_axis=0, concat_axis=0,...  97.6 us
    all_gather x1, waiting for transfers between devices, shards(): shard_rows = lax.all_gather(normed, 'node', axis=0, tiled=True)  28.8 us
    dot_general x1, matrix products, shards(): jnp.einsum('lesf,efd->lesd', hidden, w_out, preferred_element_type=jnp.fl...  25.9 us
    reduce_sum x1, other arithmetic, shards(): jnp.sum(gate_values[..., None] * picked.astype(jnp.float32), axis=2)  13.6 us
    all_to_all x1, waiting for transfers between devices, shards(): lax.all_to_all(head_results, 'node', split_axis=0, concat_axis=2, tiled=T...  11.5 us
    convert_element_type x1, local copies, waits for them, and re-layouts, shards(): partial_sum = jnp.einsum('lesf,efd->lesd', hidden, w_out, preferred_eleme...  10.8 us
    all_to_all x1, starting transfers between devices, shards(): lax.all_to_all(partial_sum, ('node', 'ep'), split_axis=0, concat_axis=0,...  10.7 us
  transfers between devices with their start and end apart: 3, of which 3 were waited for; matrix products, arithmetic and copies ran while one was open for 2% of the time, Pallas kernels for 0%

commit v1 on v0

--- a/solution.py
+++ b/solution.py
@@ -7,6 +7,19 @@
 D = 1280
 HEADS = 16
 CAP = 24
+
+
+def gather_around(array, axis, dim):
+    ways = lax.axis_size(axis)
+    up = [(d, (d + 1) % ways) for d in range(ways)]
+    down = [(d, (d - 1) % ways) for d in range(ways)]
+    earlier, later = ([array], [array])
+    for _ in range(ways // 2):
+        earlier.append(lax.ppermute(earlier[-1], axis, up))
+    for _ in range((ways - 1) // 2):
+        later.append(lax.ppermute(later[-1], axis, down))
+    line = jnp.concatenate([*earlier[::-1], *later[1:]], axis=dim)
+    return jnp.roll(line, (lax.axis_index(axis) - ways // 2) * array.shape[dim], axis=dim)
 
 
 def layer_norm(values):
@@ -32,7 +45,7 @@
     slot_count = local_images * CAP
     inputs = images.astype(jnp.float32)
     normed = layer_norm(inputs).astype(jnp.bfloat16)
-    shard_rows = lax.all_gather(normed, "node", axis=0, tiled=True)
+    shard_rows = gather_around(normed, "node", 0)
     number = shard_rows.shape[0]
     queries = jnp.einsum(
         "ctd,de->cte", shard_rows, w_query, preferred_element_type=jnp.float32

time: 397 us -> 395 us (level)
  between operations: 13.7 us -> 0.63 us
  local copies, waits for them, and re-layouts: 46.4 us -> 56.7 us
  waiting for transfers between devices: 138 us -> 132 us
    all_gather x1 -> x0, waiting for transfers between devices: 28.8 us -> none  [shards(): shard_rows = lax.all_gather(normed, 'node', axis=0, tiled=True)]
    ppermute x0 -> x3, waiting for transfers between devices: none -> 24.5 us  [the longest x2 24.5 us: gather_around(): earlier.append(lax.ppermute(earlier[-1], axis, up))]
    unnamed x15 -> x30, local copies, waits for them, and re-layouts: 0.91 us -> 9.78 us
  transfers between devices with their start and end apart: 3 -> 5, of which waited for: 3 -> 4; matrix products, arithmetic and copies ran while one was open for 2% -> 4% of each run, Pallas kernels for 0% -> 0%
where the time goes in v1:
time: 395 us; the launch traced here: 391 us
  waiting for transfers between devices  132 us (33%)
  blocking collectives  102 us (26%)
  local copies, waits for them, and re-layouts  56.7 us (14%)
  matrix products  50.9 us (13%)
  other arithmetic  31.5 us (8%)
  starting transfers between devices  17.2 us (4%)
    all_to_all x1, blocking collectives, shards(): lax.all_to_all(copies, ('node', 'ep'), split_axis=0, concat_axis=0, tiled...  102 us
    all_to_all x1, waiting for transfers between devices, shards(): lax.all_to_all(partial_sum, ('node', 'ep'), split_axis=0, concat_axis=0,...  98.2 us
    dot_general x1, matrix products, shards(): jnp.einsum('lesf,efd->lesd', hidden, w_out, preferred_element_type=jnp.fl...  25.9 us
    ppermute x2, waiting for transfers between devices, gather_around(): earlier.append(lax.ppermute(earlier[-1], axis, up))  24.5 us
    reduce_sum x1, other arithmetic, shards(): jnp.sum(gate_values[..., None] * picked.astype(jnp.float32), axis=2)  13.6 us
    convert_element_type x1, local copies, waits for them, and re-layouts, shards(): partial_sum = jnp.einsum('lesf,efd->lesd', hidden, w_out, preferred_eleme...  10.8 us
    all_to_all x1, starting transfers between devices, shards(): lax.all_to_all(partial_sum, ('node', 'ep'), split_axis=0, concat_axis=0,...  9.98 us
    unnamed x30, local copies, waits for them, and re-layouts  9.78 us
  transfers between devices with their start and end apart: 5, of which 4 were waited for; matrix products, arithmetic and copies ran while one was open for 4% of the time, Pallas kernels for 0%

profile of v1, /device:TPU:97, one launch (start us, length us, event | category | flops | bytes accessed | tf_op | source)
XLA Modules:
  0.0 391.0 jit_solution(6780929691269503147)
XLA Ops:
  5.2 2.5 collective-permute-start.2
  10.4 14.6 %collective-permute-done = bf16[1,257,1280]{2,1,0:T(8,128)(2,1)} collective-permute-done((bf16[1,257,1280]{2,1,0:T(8,128)(2,1)}, bf16[1,257,1280]{2,1,0:T(8,128)(2,1)}, u32[]{:S(2)}, u32[]{:S(2)}) %collective-permute-start) | collective-permute-done | bytes 657952 | tf_op jit(solution)/shard_map/ppermute | solution.py:18
  27.1 4.4 %scatter_custom_fusion = s32[768]{0:T(1024)S(1)} fusion(s32[514]{0:T(1024)S(1)} %fusion.64, s32[514]{0:T(1024)S(1)} %add_select_fusion, s32[]{:T(128)} %constant.106.clone.1), kind=kCustom, calls=%fused_computation.94 | custom fusion | bytes 3076 | tf_op jit(solution)/shard_map/scatter | solution.py:87
  31.5 9.9 %collective-permute-done.1 = bf16[1,257,1280]{2,1,0:T(8,128)(2,1)} collective-permute-done((bf16[1,257,1280]{2,1,0:T(8,128)(2,1)}, bf16[1,257,1280]{2,1,0:T(8,128)(2,1)}, u32[]{:S(2)}, u32[]{:S(2)}) %collective-permute-start.1) | collective-permute-done | bytes 657952 | tf_op jit(solution)/shard_map/ppermute | solution.py:18
  52.5 2.5 fusion.43
  57.3 4.6 %fusion.46 = bf16[4,257,320]{2,1,0:T(8,128)(2,1)} fusion(bf16[8,257,1280]{2,1,0:T(8,128)(2,1)} %copy-done.6, s32[]{:T(128)S(6)} %select_n.79, bf16[1280,320]{0,1:T(8,128)(2,1)} %param.11), kind=kOutput, calls=%fused_computation.45 | convolution fusion | flops 842466560 | bytes 4180484 | tf_op jit(solution)/shard_map/ctd,de->cte/dot_general | solution.py:53
  61.9 2.5 fusion.40
  69.0 6.5 %fusion.75 = (f32[4,4,257]{2,1,0:T(4,128)S(1)}, f32[4,4,257,257]{2,3,1,0:T(8,128)}) fusion(bf16[4,257,4,80]{1,3,2,0:T(8,128)(2,1)} %bitcast.109, bf16[4,257,4,80]{1,3,2,0:T(8,128)(2,1)} %bitcast.111), kind=kOutput, calls=%fused_computation.109 | convolution fusion | flops 172256048 | bytes 5559424 | tf_op jit(solution)/shard_map/sub | solution.py:65
  75.5 5.1 %fusion.39 = bf16[4,4,80,257]{3,2,1,0:T(8,128)(2,1)} fusion(bf16[4,257,4,80]{1,3,2,0:T(8,128)(2,1)} %bitcast.110, f32[4,4,257,257]{2,3,1,0:T(8,128)} %get-tuple-element.8, f32[4,4,257]{2,1,0:T(4,128)S(1)} %get-tuple-element.7), kind=kOutput, calls=%fused_computation.42 | convolution fusion | flops 171527968 | bytes 5559424 | tf_op jit(solution)/shard_map/chqk,ckhd->cqhd/dot_general | solution.py:66
  82.8 4.7 %all-to-all-start = ((bf16[4,257,320]{2,1,0:T(8,128)(2,1)}), bf16[4,257,320]{2,1,0:T(8,128)(2,1)}, u32[]{:S(2)}, u32[]{:S(2)}) async-start(bf16[4,257,320]{2,1,0:T(8,128)(2,1)} %copy.97), calls=%async_computation | async-start | bytes 1622016 | tf_op jit(solution)/shard_map/all_to_all | solution.py:72
  87.8 9.5 %all-to-all-done = bf16[4,257,320]{2,1,0:T(8,128)(2,1)} async-done(((bf16[4,257,320]{2,1,0:T(8,128)(2,1)}), bf16[4,257,320]{2,1,0:T(8,128)(2,1)}, u32[]{:S(2)}, u32[]{:S(2)}) %all-to-all-start) | async-done | bytes 657952 | tf_op jit(solution)/shard_map/all_to_all | solution.py:72
  97.3 2.3 copy.98
  99.6 2.5 reshape.358
  102.2 3.4 fusion.76
  107.7 6.4 %gather_fusion = bf16[768,1280]{1,0:T(8,128)(2,1)} fusion(bf16[257,1280]{1,0:T(8,128)(2,1)} %fusion.55, s32[1024]{0:T(1024)S(1)} %pad_clamp_fusion.1), kind=kCustom, calls=%fused_computation | custom fusion | bytes 3935232 | tf_op jit(solution)/shard_map/jit(_take)/gather | solution.py:89
  116.5 101.9 %all_to_all.25 = bf16[128,1,24,1280]{3,2,1,0:T(8,128)(2,1)} all-to-all(bf16[128,1,24,1280]{3,2,1,0:T(8,128)(2,1)S(1)} %bitcast.107), channel_id=1, replica_groups=mesh['node'=4,'ep'=32] {'node','ep'}, dimensions={0} | all-to-all | bytes 15728640 | tf_op jit(solution)/shard_map/all_to_all | solution.py:94
  218.4 25.9 %convert_bitcast_fusion = bf16[128,1,24,1280]{3,0,2,1:T(8,128)(2,1)} fusion(bf16[1,1280,1280]{2,1,0:T(8,128)(2,1)S(1)} %copy-done, bf16[128,1,24,1280]{3,2,1,0:T(8,128)(2,1)} %all_to_all.25, bf16[1,1280,1280]{2,1,0:T(8,128)(2,1)} %param.15), kind=kOutput, calls=%fused_computation.18 | convolution fusion | flops 20171980800 | bytes 22282240 | tf_op jit(solution)/shard_map/lesf,efd->lesd/dot_general | solution.py:97
  244.3 10.8 %copy.108 = bf16[128,1,24,1280]{3,2,1,0:T(8,128)(2,1)} copy(bf16[128,1,24,1280]{3,0,2,1:T(8,128)(2,1)} %convert_bitcast_fusion) | data formatting | bytes 15728640 | tf_op jit(solution)/shard_map/convert_element_type | solution.py:99
  255.1 10.0 %all-to-all-start.2 = ((bf16[128,1,24,1280]{3,2,1,0:T(8,128)(2,1)}), bf16[128,1,24,1280]{3,2,1,0:T(8,128)(2,1)}, u32[]{:S(2)}, u32[]{:S(2)}) async-start(bf16[128,1,24,1280]{3,2,1,0:T(8,128)(2,1)} %copy.108), calls=%async_computation.2 | async-start | bytes 15728640 | tf_op jit(solution)/shard_map/all_to_all | solution.py:100
  266.1 98.2 %all-to-all-done.2 = bf16[128,1,24,1280]{3,2,1,0:T(8,128)(2,1)} async-done(((bf16[128,1,24,1280]{3,2,1,0:T(8,128)(2,1)}), bf16[128,1,24,1280]{3,2,1,0:T(8,128)(2,1)}, u32[]{:S(2)}, u32[]{:S(2)}) %all-to-all-start.2) | async-done | bytes 7864352 | tf_op jit(solution)/shard_map/all_to_all | solution.py:100
  364.3 4.3 %bitcast_reduce_fusion = bf16[32,24,1280]{2,1,0:T(8,128)(2,1)S(1)} fusion(bf16[4,32,24,1280]{3,2,1,0:T(8,128)(2,1)} %bitcast.104), kind=kLoop, calls=%fused_computation.13 | loop fusion | flops 2949120 | bytes 9830400 | tf_op jit(solution)/shard_map/reduce_sum | solution.py:104
  368.6 3.5 gather_fusion.1
  372.0 4.1 %gather.15 = bf16[1,257,2,1280]{3,2,1,0:T(2,128)(2,1)} reshape(bf16[514,1280]{1,0:T(8,128)(2,1)} %gather_fusion.1) | data formatting | bytes 2631680 | tf_op jit(solution)/shard_map/jit(_take)/gather | solution.py:106
  376.2 13.6 %multiply_reduce_fusion.1 = f32[257,1280]{1,0:T(8,128)S(1)} fusion(bf16[1,257,2,1280]{3,2,1,0:T(2,128)(2,1)} %gather.15, pred[257,2]{1,0:T(8,128)(4,1)S(1)} %copy.105, f32[257,2]{1,0:T(8,128)S(1)} %copy.99), kind=kLoop, calls=%fused_computation.29 | loop fusion | flops 2302720 | bytes 2634250 | tf_op jit(solution)/shard_map/reduce_sum | solution.py:107
  (84 shorter events, 36.7 us)
Async XLA Ops:
  0.0 218.4 %copy-start = (bf16[1,1280,1280]{2,1,0:T(8,128)(2,1)S(1)}, bf16[1,1280,1280]{2,1,0:T(8,128)(2,1)}, u32[]{:S(2)}) copy-start(bf16[1,1280,1280]{2,1,0:T(8,128)(2,1)} %param.16) | copy-start | bytes 9830404
  0.0 10.4 %copy-start.9 = (s32[1,257,2]{1,2,0:T(2,128)S(1)}, s32[1,257,2]{1,2,0:T(2,128)}, u32[]{:S(2)}) copy-start(s32[1,257,2]{1,2,0:T(2,128)} %param.17) | copy-start | bytes 6172
  5.2 40.0 %collective-permute-start.2 = (bf16[1,257,1280]{2,1,0:T(8,128)(2,1)}, bf16[1,257,1280]{2,1,0:T(8,128)(2,1)}, u32[]{:S(2)}, u32[]{:S(2)}) collective-permute-start(bf16[1,257,1280]{2,1,0:T(8,128)(2,1)} %fusion.50), channel_id=1, source_target_pairs={{0,96},{32,0},{64,32},{96,64},{1,97},{33,1},{65,33},{97,65},{2,98}... | collective-permute-start | bytes 1973768 | tf_op jit(solution)/shard_map/ppermute | solution.py:20
  7.6 17.3 %collective-permute-start = (bf16[1,257,1280]{2,1,0:T(8,128)(2,1)}, bf16[1,257,1280]{2,1,0:T(8,128)(2,1)}, u32[]{:S(2)}, u32[]{:S(2)}) collective-permute-start(bf16[1,257,1280]{2,1,0:T(8,128)(2,1)} %fusion.50), channel_id=1, source_target_pairs={{0,32},{32,64},{64,96},{96,0},{1,33},{33,65},{65,97},{97,1},{2,34}... | collective-permute-start | bytes 1973768 | tf_op jit(solution)/shard_map/ppermute | solution.py:18
  24.9 16.4 %collective-permute-start.1 = (bf16[1,257,1280]{2,1,0:T(8,128)(2,1)}, bf16[1,257,1280]{2,1,0:T(8,128)(2,1)}, u32[]{:S(2)}, u32[]{:S(2)}) collective-permute-start(bf16[1,257,1280]{2,1,0:T(8,128)(2,1)} %collective-permute-done), channel_id=1, source_target_pairs={{0,32},{32,64},{64,96},{96,0},{1,33},{33,65},{65,97},{97,1},{2,34}... | collective-permute-start | bytes 1973768 | tf_op jit(solution)/shard_map/ppermute | solution.py:18
  42.5 6.2 %copy-start.3 = (bf16[1,257,1280]{2,1,0:T(8,128)(2,1)S(1)}, bf16[1,257,1280]{2,1,0:T(8,128)(2,1)}, u32[]{:S(2)}) copy-start(bf16[1,257,1280]{2,1,0:T(8,128)(2,1)} %param.9) | copy-start | bytes 1973764
  45.2 7.3 %copy-start.10 = (bf16[1280,320]{0,1:T(8,128)(2,1)S(1)}, bf16[1280,320]{0,1:T(8,128)(2,1)}, u32[]{:S(2)}) copy-start(bf16[1280,320]{0,1:T(8,128)(2,1)} %param.10) | copy-start | bytes 2457604
  50.2 2.3 copy-start.6
  57.3 4.6 %copy-start.7 = (bf16[8,257,1280]{2,1,0:T(8,128)(2,1)S(1)}, bf16[8,257,1280]{2,1,0:T(8,128)(2,1)}, u32[]{:S(2)}) copy-start(bf16[8,257,1280]{2,1,0:T(8,128)(2,1)} %copy-done.6) | copy-start | bytes 15790084
  57.3 4.6 %copy-start.11 = (bf16[1280,320]{0,1:T(8,128)(2,1)S(1)}, bf16[1280,320]{0,1:T(8,128)(2,1)}, u32[]{:S(2)}) copy-start(bf16[1280,320]{0,1:T(8,128)(2,1)} %param.12) | copy-start | bytes 2457604
  82.8 14.5 %all-to-all-start = ((bf16[4,257,320]{2,1,0:T(8,128)(2,1)}), bf16[4,257,320]{2,1,0:T(8,128)(2,1)}, u32[]{:S(2)}, u32[]{:S(2)}) async-start(bf16[4,257,320]{2,1,0:T(8,128)(2,1)} %copy.97), calls=%async_computation | async-start | bytes 1622016 | tf_op jit(solution)/shard_map/all_to_all | solution.py:72
  105.6 1.1 copy-start.4
  255.1 10.5 %copy-start.2 = (bf16[257,1280]{1,0:T(8,128)(2,1)S(1)}, bf16[257,1280]{1,0:T(8,128)(2,1)}, u32[]{:S(2)}) copy-start(bf16[257,1280]{1,0:T(8,128)(2,1)} %fusion.55) | copy-start | bytes 1973764
  255.1 10.5 %copy-start.8 = (bf16[1280,32]{0,1:T(8,128)(2,1)S(1)}, bf16[1280,32]{0,1:T(8,128)(2,1)}, u32[]{:S(2)}) copy-start(bf16[1280,32]{0,1:T(8,128)(2,1)} %param.14) | copy-start | bytes 245764
  255.1 109.2 %all-to-all-start.2 = ((bf16[128,1,24,1280]{3,2,1,0:T(8,128)(2,1)}), bf16[128,1,24,1280]{3,2,1,0:T(8,128)(2,1)}, u32[]{:S(2)}, u32[]{:S(2)}) async-start(bf16[128,1,24,1280]{3,2,1,0:T(8,128)(2,1)} %copy.108), calls=%async_computation.2 | async-start | bytes 15728640 | tf_op jit(solution)/shard_map/all_to_all | solution.py:100
  372.0 18.7 %copy-start.1 = (bf16[1,1280,1280]{2,1,0:T(8,128)(2,1)S(1)}, bf16[1,1280,1280]{2,1,0:T(8,128)(2,1)}, u32[]{:S(2)}) copy-start(bf16[1,1280,1280]{2,1,0:T(8,128)(2,1)} %param.16) | copy-start | bytes 9830404
  376.2 13.6 %copy-start.5 = (f32[1,257,1280]{2,1,0:T(8,128)S(1)}, f32[1,257,1280]{2,1,0:T(8,128)}, u32[]{:S(2)}) copy-start(f32[1,257,1280]{2,1,0:T(8,128)} %copy-done.4) | copy-start | bytes 3947524
